TPU v7x, 256 devices: a whole 4x4x8 slice. The times are simulated.
256 devices in a mesh: ctx: 64 (over z, x_hi, y), hd: 4 (over x_lo, core).
Axes of the slice: x: 4 (x_hi: 2, x_lo: 2; x = x_hi * 2 + x_lo), y: 4, z: 8, core: 2. Of those that a mesh axis runs over, the one named last changes fastest.
Arguments:
- tokens: bfloat16 [32768, 4096], P('ctx'), may hold values from -6 to 6
- w_query: bfloat16 [4096, 2048], P('ctx', 'hd'), may hold values from -0.09375 to 0.09375
- w_key: bfloat16 [4096, 2048], P('ctx', 'hd'), may hold values from -0.09375 to 0.09375
- w_value: bfloat16 [4096, 2048], P('ctx', 'hd'), may hold values from -0.09375 to 0.09375
Outputs:
- attended: bfloat16 [32768, 2048], P('ctx', 'hd')
All inputs are finite; a program needn't handle non-finite values.
Results may differ from a plain program's by a relative error of at most 0.0065.
Values may be sent and summed in bfloat16 or wider, within the bound.
No kernel may reach another device: no remote copies, remote signals or barrier semaphores. Data moves between devices by JAX's collectives and lax.ppermute only.
A program may use at most 64 MiB of HBM per device.

v0:
```python
import jax
import jax.numpy as jnp
from jax import lax
from jax.sharding import PartitionSpec as P

DH = 128
BLOCK = 512
epsilon = 1e-06


def carried_in(part, axis, combine, identity):
    place = lax.axis_index(axis)
    gathered = lax.all_gather(part, axis)
    state = jnp.zeros_like(part) + jnp.asarray(identity, part.dtype)

    def one(hop, state):
        return combine(state, lax.dynamic_index_in_dim(gathered, hop, 0, False))

    return lax.fori_loop(0, place, one, state)


def local(tokens, w_query, w_key, w_value):
    tok_rows = tokens.shape[0]
    width_group = w_query.shape[1]
    head_count = width_group // DH
    block_count = tok_rows // BLOCK
    query_full = jnp.dot(
        tokens,
        lax.all_gather(w_query, "ctx", axis=0, tiled=True),
        preferred_element_type=jnp.float32,
    )
    key_full = jnp.dot(
        tokens, lax.all_gather(w_key, "ctx", axis=0, tiled=True), preferred_element_type=jnp.float32
    )
    value_full = jnp.dot(
        tokens,
        lax.all_gather(w_value, "ctx", axis=0, tiled=True),
        preferred_element_type=jnp.float32,
    )
    query_rows = query_full.astype(jnp.bfloat16).reshape(block_count, BLOCK, head_count, DH)
    key_rows = key_full.astype(jnp.bfloat16).reshape(block_count, BLOCK, head_count, DH)
    value_rows = value_full.astype(jnp.bfloat16).reshape(block_count, BLOCK, head_count, DH)
    causal_mask = jnp.tril(jnp.ones((BLOCK, BLOCK), dtype=bool))
    scores = jnp.einsum("bqhd,bkhd->bhqk", query_rows, key_rows, preferred_element_type=jnp.float32)
    scores = jnp.where(causal_mask[None, None], scores, 0.0).astype(jnp.bfloat16)
    local_term = jnp.einsum(
        "bhqk,bkhd->bqhd", scores, value_rows, preferred_element_type=jnp.float32
    )
    block_states = jnp.einsum(
        "bkhd,bkhe->bhde", key_rows, value_rows, preferred_element_type=jnp.float32
    )
    own_total = jnp.sum(block_states, axis=0)

    def add_states(earlier, later_part):
        return earlier + later_part

    prefix_state = carried_in(own_total, "ctx", add_states, jnp.zeros_like(own_total))
    before_blocks = jnp.concatenate([jnp.zeros_like(block_states), block_states[:-1]], axis=0)
    start_states = prefix_state[None] + jnp.cumsum(before_blocks, axis=0)
    carried = jnp.einsum(
        "bqhd,bhde->bqhe",
        query_rows.astype(jnp.float32),
        start_states,
        precision=lax.Precision.HIGHEST,
    )
    attended_raw = carried + local_term
    scale_inv = lax.rsqrt(jnp.mean(attended_raw * attended_raw, axis=-1, keepdims=True) + epsilon)
    return (attended_raw * scale_inv).astype(jnp.bfloat16).reshape(tok_rows, width_group)


def solution(mesh):
    return jax.shard_map(
        local,
        mesh=mesh,
        in_specs=(P("ctx", None), P("ctx", "hd"), P("ctx", "hd"), P("ctx", "hd")),
        out_specs=P("ctx", "hd"),
        check_vma=False,
    )
```

profile of v0, /device:TPU:254, one launch (start us, length us, event | category | flops | bytes accessed | tf_op | source)
XLA Modules:
  0.0 674.8 jit_solution(13655943641388664750)
XLA Ops:
  8.8 126.3 %all-gather.6.cloned.1.call-done = bf16[4096,512]{1,0:T(8,128)(2,1)} async-done(((bf16[64,512]{1,0:T(8,128)(2,1)}), bf16[4096,512]{1,0:T(8,128)(2,1)}) %all-gather.6.cloned.1.call-update) | async-done | bytes 4194320 | tf_op jit(solution)/shard_map/all_gather | solution.py:33
  135.0 5.8 convolution_convert_fusion.2
  140.9 121.8 %all-gather.8.cloned.1.call-done = bf16[4096,512]{1,0:T(8,128)(2,1)} async-done(((bf16[64,512]{1,0:T(8,128)(2,1)}), bf16[4096,512]{1,0:T(8,128)(2,1)}) %all-gather.8.cloned.1.call-update) | async-done | bytes 4194320 | tf_op jit(solution)/shard_map/all_gather | solution.py:37
  262.7 5.8 convolution_convert_fusion.1
  270.5 119.9 %all-gather.10.cloned.1.call-done = bf16[4096,512]{1,0:T(8,128)(2,1)} async-done(((bf16[64,512]{1,0:T(8,128)(2,1)}), bf16[4096,512]{1,0:T(8,128)(2,1)}) %all-gather.10.cloned.1.call-update) | async-done | bytes 4194320 | tf_op jit(solution)/shard_map/all_gather | solution.py:29
  390.4 5.8 convolution_convert_fusion
  396.2 202.4 %all-gather.12.cloned.1.call-done = f32[256,128,128]{2,1,0:T(8,128)} async-done(((f32[4,128,128]{2,1,0:T(8,128)}), f32[256,128,128]{2,1,0:T(8,128)}) %all-gather.12.cloned.1.call-update) | async-done | bytes 16777232 | tf_op jit(solution)/shard_map/all_gather | solution.py:13
  598.6 65.4 %while.10 = (s32[]{:T(128)}, f32[4,128,128]{2,1,0:T(8,128)S(1)}, s32[]{:T(128)}, f32[64,4,128,128]{3,2,1,0:T(8,128)}, s32[]{:T(128)}, /*index=5*/s32[]{:T(128)}, s32[]{:T(128)}) while((s32[]{:T(128)}, f32[4,128,128]{2,1,0:T(8,128)S(1)}, s32[]{:T(128)}, f32[64,4,128,128]{3,2,1,0:T(8,128)}, s32[]{:T(128)}, /*index=5*/s32[]{:T(128)}, ...), condition=%wide.region_1.2_spmd, body=%wide.region_0.1_spmd.sunk | while | flops 65541 | bytes 786547 | solution.py:19
  598.6 1.0 bitcast_add_fusion.2
  599.6 1.0 bitcast_add_fusion.2
  600.7 1.0 bitcast_add_fusion.2
  601.7 1.0 bitcast_add_fusion.2
  602.7 1.0 bitcast_add_fusion.2
  603.8 1.0 bitcast_add_fusion.2
  604.8 1.0 bitcast_add_fusion.2
  605.9 1.0 bitcast_add_fusion.2
  606.9 1.0 bitcast_add_fusion.2
  607.9 1.0 bitcast_add_fusion.2
  609.0 1.0 bitcast_add_fusion.2
  610.0 1.0 bitcast_add_fusion.2
  611.1 1.0 bitcast_add_fusion.2
  612.1 1.0 bitcast_add_fusion.2
  613.1 1.0 bitcast_add_fusion.2
  614.2 1.0 bitcast_add_fusion.2
  615.2 1.0 bitcast_add_fusion.2
  616.2 1.0 bitcast_add_fusion.2
  617.3 1.0 bitcast_add_fusion.2
  618.3 1.0 bitcast_add_fusion.2
  619.4 1.0 bitcast_add_fusion.2
  620.4 1.0 bitcast_add_fusion.2
  621.4 1.0 bitcast_add_fusion.2
  622.5 1.0 bitcast_add_fusion.2
  623.5 1.0 bitcast_add_fusion.2
  624.5 1.0 bitcast_add_fusion.2
  625.6 1.0 bitcast_add_fusion.2
  626.6 1.0 bitcast_add_fusion.2
  630.8 1.0 bitcast_add_fusion.2
  634.9 1.0 bitcast_add_fusion.2
  638.0 1.0 bitcast_add_fusion.2
  639.1 1.0 bitcast_add_fusion.2
  642.2 1.0 bitcast_add_fusion.2
  646.3 1.0 bitcast_add_fusion.2
  650.5 1.0 bitcast_add_fusion.2
  654.6 1.0 bitcast_add_fusion.2
  657.8 1.0 bitcast_add_fusion.2
  658.8 1.0 bitcast_add_fusion.2
  661.9 1.0 bitcast_add_fusion.2
  664.6 2.5 multiply_reduce_fusion
  (41 shorter events, 30.1 us)
Async XLA Ops:
  6.5 128.5 %all-gather.6.cloned.1.call-start = ((), (), s32[]{:S(2)}) async-start(), calls=%async_computation | async-start | bytes 4259840 | tf_op jit(solution)/shard_map/all_gather | solution.py:33
  7.3 255.4 %all-gather.8.cloned.1.call-start = ((), (), s32[]{:S(2)}) async-start(), calls=%async_computation.1 | async-start | bytes 4259840 | tf_op jit(solution)/shard_map/all_gather | solution.py:37
  8.0 382.4 %all-gather.10.cloned.1.call-start = ((), (), s32[]{:S(2)}) async-start(), calls=%async_computation.2 | async-start | bytes 4259840 | tf_op jit(solution)/shard_map/all_gather | solution.py:29
  8.7 589.8 %all-gather.12.cloned.1.call-start = ((), (), s32[]{:S(2)}) async-start(), calls=%async_computation.3 | async-start | bytes 17039360 | tf_op jit(solution)/shard_map/all_gather | solution.py:13
  268.5 0.8 copy-start
Sparse Core Ops, SparseCore 0:
  10.8 124.1 all-gather.5
  138.5 124.1 all-gather.7
  266.2 124.1 all-gather.9
  393.7 204.8 all-gather.11
where the time goes:
time: 677 us; the launch traced here: 675 us
  waiting for transfers between devices  572 us (84%)
  other arithmetic  63.9 us (9%)
  matrix products  21.6 us (3%)
  between operations  13.2 us (2%)
    all_gather x1, waiting for transfers between devices, carried_in(): gathered = lax.all_gather(part, axis)  202 us
    all_gather x1, waiting for transfers between devices, local(): lax.all_gather(w_key, 'ctx', axis=0, tiled=True)  126 us
    all_gather x1, waiting for transfers between devices, local(): lax.all_gather(w_value, 'ctx', axis=0, tiled=True)  122 us
    all_gather x1, waiting for transfers between devices, local(): lax.all_gather(w_query, 'ctx', axis=0, tiled=True)  120 us
    add x63, other arithmetic, add_states(): return earlier + later_part  63.7 us
  transfers between devices with their start and end apart: 4, of which 4 were waited for; matrix products, arithmetic and copies ran while one was open for 3% of the time, Pallas kernels for 0%

commit v1 on v0

--- a/solution.py
+++ b/solution.py
@@ -30,7 +30,11 @@
         preferred_element_type=jnp.float32,
     )
     key_full = jnp.dot(
-        tokens, lax.all_gather(w_key, "ctx", axis=0, tiled=True), preferred_element_type=jnp.float32
+        tokens,
+        jnp.concatenate(
+            lax.all_to_all(jnp.stack([w_key] * lax.axis_size("ctx")), "ctx", 0, 0), axis=0
+        ),
+        preferred_element_type=jnp.float32,
     )
     value_full = jnp.dot(
         tokens,

time: 677 us -> 569 us (0.84)
  waiting for transfers between devices: 572 us -> 449 us
  starting transfers between devices: 0.12 us -> 11.7 us
    all_gather x1 -> x0, waiting for transfers between devices: 126 us -> none  [local(): lax.all_gather(w_key, 'ctx', axis=0, tiled=True)]
    all_to_all x0 -> x1, waiting for transfers between devices: none -> 101 us  [local(): lax.all_to_all(jnp.stack([w_key] * lax.axis_size('ctx')), 'ctx', 0, 0)]
    all_gather x1, waiting for transfers between devices: 122 us -> 23.2 us  [local(): lax.all_gather(w_value, 'ctx', axis=0, tiled=True)]
    all_to_all x0 -> x1, starting transfers between devices: none -> 11.6 us  [local(): lax.all_to_all(jnp.stack([w_key] * lax.axis_size('ctx')), 'ctx', 0, 0)]
  transfers between devices with their start and end apart: 4 -> 4, of which waited for: 4 -> 4; matrix products, arithmetic and copies ran while one was open for 3% -> 4% of each run, Pallas kernels for 0% -> 0%
where the time goes in v1:
time: 569 us; the launch traced here: 567 us
  waiting for transfers between devices  449 us (79%)
  other arithmetic  63.9 us (11%)
  matrix products  21.7 us (4%)
  between operations  13.2 us (2%)
  starting transfers between devices  11.7 us (2%)
    all_gather x1, waiting for transfers between devices, carried_in(): gathered = lax.all_gather(part, axis)  203 us
    all_gather x1, waiting for transfers between devices, local(): lax.all_gather(w_query, 'ctx', axis=0, tiled=True)  121 us
    all_to_all x1, waiting for transfers between devices, local(): lax.all_to_all(jnp.stack([w_key] * lax.axis_size('ctx')), 'ctx', 0, 0)  101 us
    add x63, other arithmetic, add_states(): return earlier + later_part  63.7 us
    all_gather x1, waiting for transfers between devices, local(): lax.all_gather(w_value, 'ctx', axis=0, tiled=True)  23.2 us
    all_to_all x1, starting transfers between devices, local(): lax.all_to_all(jnp.stack([w_key] * lax.axis_size('ctx')), 'ctx', 0, 0)  11.6 us
  transfers between devices with their start and end apart: 4, of which 4 were waited for; matrix products, arithmetic and copies ran while one was open for 4% of the time, Pallas kernels for 0%

profile of v1, /device:TPU:254, one launch (start us, length us, event | category | flops | bytes accessed | tf_op | source)
XLA Modules:
  0.0 566.6 jit_solution(807263348547113832)
XLA Ops:
  7.3 3.3 stack.2
  10.6 11.6 %all-to-all-start = ((bf16[64,64,512]{2,1,0:T(8,128)(2,1)}), bf16[64,64,512]{2,1,0:T(8,128)(2,1)}, u32[]{:S(2)}, u32[]{:S(2)}) async-start(bf16[64,64,512]{2,1,0:T(8,128)(2,1)} %stack.2), calls=%async_computation | async-start | bytes 8388608 | tf_op jit(solution)/shard_map/all_to_all | solution.py:35
  23.0 101.5 %all-to-all-done = bf16[64,64,512]{2,1,0:T(8,128)(2,1)} async-done(((bf16[64,64,512]{2,1,0:T(8,128)(2,1)}), bf16[64,64,512]{2,1,0:T(8,128)(2,1)}, u32[]{:S(2)}, u32[]{:S(2)}) %all-to-all-start) | async-done | bytes 4194336 | tf_op jit(solution)/shard_map/all_to_all | solution.py:35
  124.5 5.9 %convolution_convert_fusion.2 = bf16[512,512]{0,1:T(8,128)(2,1)S(1)} fusion(bf16[512,4096]{1,0:T(8,128)(2,1)} %param.6, bf16[4096,512]{1,0:T(8,128)(2,1)} %bitcast.1), kind=kOutput, calls=%fused_computation.7 | convolution fusion | flops 2147745792 | bytes 8912896 | tf_op jit(solution)/shard_map/dot_general | solution.py:32
  130.3 23.2 %all-gather.5.cloned.1.call-done = bf16[4096,512]{1,0:T(8,128)(2,1)} async-done(((bf16[64,512]{1,0:T(8,128)(2,1)}), bf16[4096,512]{1,0:T(8,128)(2,1)}) %all-gather.5.cloned.1.call-update) | async-done | bytes 4194320 | tf_op jit(solution)/shard_map/all_gather | solution.py:41
  153.5 5.8 %convolution_convert_fusion.1 = bf16[512,512]{0,1:T(8,128)(2,1)S(1)} fusion(bf16[512,4096]{1,0:T(8,128)(2,1)} %param.6, bf16[4096,512]{1,0:T(8,128)(2,1)} %all-gather.5.cloned.1.call-done), kind=kOutput, calls=%fused_computation.6 | convolution fusion | flops 2147745792 | bytes 8912896 | tf_op jit(solution)/shard_map/dot_general | solution.py:39
  161.3 120.7 %all-gather.7.cloned.1.call-done = bf16[4096,512]{1,0:T(8,128)(2,1)} async-done(((bf16[64,512]{1,0:T(8,128)(2,1)}), bf16[4096,512]{1,0:T(8,128)(2,1)}) %all-gather.7.cloned.1.call-update) | async-done | bytes 4194320 | tf_op jit(solution)/shard_map/all_gather | solution.py:29
  282.0 5.8 %convolution_convert_fusion = bf16[512,512]{0,1:T(8,128)(2,1)S(1)} fusion(bf16[512,4096]{1,0:T(8,128)(2,1)} %param.6, bf16[4096,512]{1,0:T(8,128)(2,1)} %all-gather.7.cloned.1.call-done), kind=kOutput, calls=%fused_computation.5 | convolution fusion | flops 2147745792 | bytes 8912896 | tf_op jit(solution)/shard_map/dot_general | solution.py:27
  287.9 202.5 %all-gather.9.cloned.1.call-done = f32[256,128,128]{2,1,0:T(8,128)} async-done(((f32[4,128,128]{2,1,0:T(8,128)}), f32[256,128,128]{2,1,0:T(8,128)}) %all-gather.9.cloned.1.call-update) | async-done | bytes 16777232 | tf_op jit(solution)/shard_map/all_gather | solution.py:13
  490.4 65.4 %while.10 = (s32[]{:T(128)}, f32[4,128,128]{2,1,0:T(8,128)S(1)}, s32[]{:T(128)}, f32[64,4,128,128]{3,2,1,0:T(8,128)}, s32[]{:T(128)}, /*index=5*/s32[]{:T(128)}, s32[]{:T(128)}) while((s32[]{:T(128)}, f32[4,128,128]{2,1,0:T(8,128)S(1)}, s32[]{:T(128)}, f32[64,4,128,128]{3,2,1,0:T(8,128)}, s32[]{:T(128)}, /*index=5*/s32[]{:T(128)}, ...), condition=%wide.region_1.2_spmd, body=%wide.region_0.1_spmd.sunk | while | flops 65541 | bytes 786547 | solution.py:19
  490.4 1.0 bitcast_add_fusion.2
  491.5 1.0 bitcast_add_fusion.2
  492.5 1.0 bitcast_add_fusion.2
  493.5 1.0 bitcast_add_fusion.2
  494.6 1.0 bitcast_add_fusion.2
  495.6 1.0 bitcast_add_fusion.2
  496.7 1.0 bitcast_add_fusion.2
  497.7 1.0 bitcast_add_fusion.2
  498.7 1.0 bitcast_add_fusion.2
  499.8 1.0 bitcast_add_fusion.2
  500.8 1.0 bitcast_add_fusion.2
  501.8 1.0 bitcast_add_fusion.2
  502.9 1.0 bitcast_add_fusion.2
  503.9 1.0 bitcast_add_fusion.2
  505.0 1.0 bitcast_add_fusion.2
  506.0 1.0 bitcast_add_fusion.2
  507.0 1.0 bitcast_add_fusion.2
  508.1 1.0 bitcast_add_fusion.2
  509.1 1.0 bitcast_add_fusion.2
  510.1 1.0 bitcast_add_fusion.2
  511.2 1.0 bitcast_add_fusion.2
  512.2 1.0 bitcast_add_fusion.2
  513.3 1.0 bitcast_add_fusion.2
  514.3 1.0 bitcast_add_fusion.2
  515.3 1.0 bitcast_add_fusion.2
  518.5 1.0 bitcast_add_fusion.2
  522.6 1.0 bitcast_add_fusion.2
  525.7 1.0 bitcast_add_fusion.2
  526.8 1.0 bitcast_add_fusion.2
  529.9 1.0 bitcast_add_fusion.2
  534.0 1.0 bitcast_add_fusion.2
  538.2 1.0 bitcast_add_fusion.2
  542.3 1.0 bitcast_add_fusion.2
  545.4 1.0 bitcast_add_fusion.2
  546.5 1.0 bitcast_add_fusion.2
  549.6 1.0 bitcast_add_fusion.2
  553.7 1.0 bitcast_add_fusion.2
  556.4 2.5 multiply_reduce_fusion
  (41 shorter events, 31.4 us)
Async XLA Ops:
  6.5 147.0 %all-gather.5.cloned.1.call-start = ((), (), s32[]{:S(2)}) async-start(), calls=%async_computation.1 | async-start | bytes 4259840 | tf_op jit(solution)/shard_map/all_gather | solution.py:41
  10.6 113.9 %all-to-all-start = ((bf16[64,64,512]{2,1,0:T(8,128)(2,1)}), bf16[64,64,512]{2,1,0:T(8,128)(2,1)}, u32[]{:S(2)}, u32[]{:S(2)}) async-start(bf16[64,64,512]{2,1,0:T(8,128)(2,1)} %stack.2), calls=%async_computation | async-start | bytes 8388608 | tf_op jit(solution)/shard_map/all_to_all | solution.py:35
  22.2 259.9 %all-gather.7.cloned.1.call-start = ((), (), s32[]{:S(2)}) async-start(), calls=%async_computation.2 | async-start | bytes 4259840 | tf_op jit(solution)/shard_map/all_gather | solution.py:29
  22.9 467.5 %all-gather.9.cloned.1.call-start = ((), (), s32[]{:S(2)}) async-start(), calls=%async_computation.3 | async-start | bytes 17039360 | tf_op jit(solution)/shard_map/all_gather | solution.py:13
  159.4 0.8 copy-start
Sparse Core Ops, SparseCore 0:
  10.8 142.6 all-gather.4
  157.0 124.9 all-gather.6
  285.5 204.8 all-gather.8
